TPU v7x, 512 devices: a whole 4x8x8 slice. The times are simulated.
512 devices in a mesh: row: 16 (over z, core), col: 32 (over y, x).
Axes of the slice: x: 4, y: 8, z: 8, core: 2. Of those that a mesh axis runs over, the one named last changes fastest.
Arguments:
- a11: float32 [256, 256], replicated, may hold values from -1 to 400, as said below
- l11_bar: float32 [256, 256], replicated, may hold values from -24 to 24
- a21: float32 [32768, 256], P(('col', 'row')), may hold values from -72 to 72
- l21_bar: float32 [32768, 256], P(('col', 'row')), may hold values from -6 to 6
- s_bar: bfloat16 [32, 16, 64, 32768], P(None, 'row', None, 'col'), may hold values from -0.0625 to 0.0625
Outputs:
- a21_bar: float32 [32768, 256], P(('col', 'row'))
- a11_bar: float32 [256, 256], replicated
Inputs may be any that keep to these rules, and one draw needn't show every extreme that they name: a11 is symmetric and each diagonal entry exceeds the sum of the magnitudes of the other entries of its row.
All inputs are finite; a program needn't handle non-finite values.
Results may differ from a plain program's by a relative error of at most 0.0036.
Values may be sent and summed in bfloat16 or wider, within the bound.
No kernel may reach another device: no remote copies, remote signals or barrier semaphores. Data moves between devices by JAX's collectives and lax.ppermute only.
A program may use at most 64 MiB of HBM per device.

v0:
```python
import jax
import jax.numpy as jnp
from jax import lax
from jax.sharding import PartitionSpec as P


def halve_lower(square):
    lower = jnp.tril(square)
    return lower - 0.5 * jnp.diag(jnp.diag(square))


def right_solve_t(factor, rhs):
    return lax.linalg.triangular_solve(factor, rhs, left_side=False, lower=True, transpose_a=True)


def right_solve(factor, rhs):
    return lax.linalg.triangular_solve(factor, rhs, left_side=False, lower=True, transpose_a=False)


def left_solve_t(factor, rhs):
    return lax.linalg.triangular_solve(factor, rhs, left_side=True, lower=True, transpose_a=True)


def inner_rows(left, right):
    return lax.dot_general(
        left, right, (((0,), (0,)), ((), ())), preferred_element_type=jnp.float32
    )


def body(a11, l11_bar, a21, l21_bar, s_bar):
    highest = lax.Precision.HIGHEST
    rows_own = a21.shape[0]
    blocks_here = s_bar.shape[0]
    tile = s_bar.reshape(blocks_here * rows_own, s_bar.shape[3])
    l11 = jnp.linalg.cholesky(a11)
    l21_own = right_solve_t(l11, a21)
    panel_own = l21_own.astype(jnp.bfloat16)
    panel_rows = lax.all_gather(panel_own, "col", axis=0, tiled=True)
    panel_cols = lax.all_gather(panel_own, "row", axis=0, tiled=True)
    strip = tile
    row_share = lax.psum_scatter(
        jnp.dot(strip, panel_cols, preferred_element_type=jnp.float32),
        "col",
        scatter_dimension=0,
        tiled=True,
    )
    strip = tile
    col_share = lax.psum_scatter(
        inner_rows(strip, panel_rows), "row", scatter_dimension=0, tiled=True
    )
    trail = l21_bar - row_share - col_share
    a21_bar = right_solve(l11, trail)
    panel_exact = panel_own.astype(jnp.float32)
    coupling = lax.psum(jnp.dot(trail.T, panel_exact, precision=highest), ("row", "col"))
    l11_total = l11_bar - left_solve_t(l11, coupling)
    middle = halve_lower(jnp.dot(l11.T, l11_total, precision=highest))
    left = left_solve_t(l11, middle)
    whole = right_solve(l11, left)
    a11_bar = 0.5 * (whole + whole.T)
    return (a21_bar, a11_bar)


def solution(mesh):
    in_specs = (
        P(),
        P(),
        P(("col", "row"), None),
        P(("col", "row"), None),
        P(None, "row", None, "col"),
    )
    out_specs = (P(("col", "row"), None), P())
    return jax.shard_map(body, mesh=mesh, in_specs=in_specs, out_specs=out_specs, check_vma=False)
```

profile of v0, /device:TPU:23, one launch (start us, length us, event | category | flops | bytes accessed | tf_op | source)
XLA Modules:
  0.0 740.2 jit_solution(10154742874111276805)
XLA Ops:
  7.2 1.1 copy.13
  8.3 1.0 fusion.4
  9.3 11.7 %cholesky.50 = f32[128,128]{1,0:T(8,128)S(1)} custom-call(f32[128,128]{1,0:T(8,128)S(1)} %cholesky.118), custom_call_target="Cholesky" | custom-call | tf_op jit(solution)/shard_map/jit(cholesky)/cholesky | solution.py:35
  21.1 9.8 %custom-call.21 = f32[1,128,128]{1,2,0:T(8,128)S(1)} custom-call(f32[1,128,128]{2,1,0:T(8,128)S(1)} %get-tuple-element.40), custom_call_target="InvertDiagBlocksLowerTriangular" | custom-call | tf_op jit(solution)/shard_map/jit(cholesky)/cholesky | solution.py:35
  30.9 0.2 constant_dynamic-update-slice_fusion.1
  31.1 0.3 convolution_subtract_fusion.3
  31.4 11.7 %cholesky.105 = f32[128,128]{1,0:T(8,128)S(1)} custom-call(f32[128,128]{1,0:T(8,128)S(1)} %convolution_subtract_fusion.3), custom_call_target="Cholesky" | custom-call | tf_op jit(solution)/shard_map/jit(cholesky)/cholesky | solution.py:35
  43.1 0.6 compare_reduce_fusion
  45.0 0.1 triangular_solve.101
  45.1 4.0 while.5
  45.3 0.6 fusion.56
  45.8 1.3 bitcast_dynamic-update-slice_fusion.2
  47.2 0.6 fusion.56
  47.8 1.3 bitcast_dynamic-update-slice_fusion.2
  49.1 19.7 %custom-call.22 = f32[2,128,128]{1,2,0:T(8,128)S(1)} custom-call(f32[2,128,128]{2,1,0:T(8,128)S(1)} %get-tuple-element.18), custom_call_target="InvertDiagBlocksLowerTriangular" | custom-call | tf_op jit(solution)/shard_map/triangular_solve | solution.py:13
  68.7 0.9 fusion.23
  69.7 1.0 convolution_subtract_fusion.5
  70.7 0.2 convolution_convert_fusion
  70.9 0.6 pad_maximum_fusion.4
  71.6 79.2 %all-gather.2.cloned.1.call-done = bf16[2048,256]{1,0:T(8,128)(2,1)} async-done(((bf16[64,256]{1,0:T(8,128)(2,1)}), bf16[2048,256]{1,0:T(8,128)(2,1)}) %all-gather.2.cloned.1.call-update) | async-done | bytes 1048592 | tf_op jit(solution)/shard_map/all_gather | solution.py:38
  150.8 3.8 convolution_bitcast_fusion.1
  154.6 1.3 copy.19
  156.0 25.2 %all_gather.6 = bf16[1024,256]{1,0:T(8,128)(2,1)S(1)} all-gather(bf16[64,256]{1,0:T(8,128)(2,1)S(1)} %copy-done), channel_id=1, replica_groups=mesh['row'=16,'col'=32] {'row'}, dimensions={0}, use_global_device_ids=true | all-gather | bytes 557056 | tf_op jit(solution)/shard_map/all_gather | solution.py:39
  181.2 3.5 convolution_bitcast_fusion
  184.8 1.9 copy.17
  186.7 33.0 %reduce-scatter.9.cloned.1.call-done = f32[64,256]{1,0:T(8,128)} async-done(((f32[1024,256]{1,0:T(8,128)}), f32[64,256]{1,0:T(8,128)}) %reduce-scatter.9.cloned.1.call-update) | async-done | bytes 65552 | tf_op jit(solution)/shard_map/reduce_scatter | solution.py:48
  219.7 222.1 %reduce-scatter.7.cloned.1.call-done = f32[64,256]{1,0:T(8,128)} async-done(((f32[2048,256]{1,0:T(8,128)}), f32[64,256]{1,0:T(8,128)}) %reduce-scatter.7.cloned.1.call-update) | async-done | bytes 65552 | tf_op jit(solution)/shard_map/reduce_scatter | solution.py:41
  441.8 0.9 subtract_subtract_fusion
  442.7 1.0 fusion.36
  443.7 0.2 fusion.24
  444.0 0.2 convolution_subtract_fusion.4
  444.2 0.2 fusion.22
  444.4 0.6 pad_maximum_fusion.3
  445.1 280.3 %all-reduce.3.cloned.1.call-done = f32[256,256]{1,0:T(8,128)} async-done(((f32[256,256]{1,0:T(8,128)}), f32[256,256]{1,0:T(8,128)}) %all-reduce.3.cloned.1.call-update) | async-done | bytes 262160 | tf_op jit(solution)/shard_map/psum | solution.py:54
  725.3 1.2 fusion.11
  726.5 1.2 convolution_subtract_fusion.2
  727.7 0.3 fusion.19
  728.0 0.5 fusion
  728.5 2.3 gather_fusion
  730.9 0.1 multiply_subtract_fusion
  731.0 0.3 fusion.9
  731.2 0.3 convolution_subtract_fusion.1
  731.6 0.3 fusion.20
  731.8 0.3 fusion.7
  732.1 0.4 convolution_subtract_fusion
  732.5 0.3 fusion.21
  732.8 0.1 copy.16
  733.0 0.7 fusion.3
  (26 shorter events, 0.4 us)
Async XLA Ops:
  7.2 143.7 %all-gather.2.cloned.1.call-start = ((), (), s32[]{:S(2)}) async-start(), calls=%async_computation.2 | async-start | bytes 1081344 | tf_op jit(solution)/shard_map/all_gather | solution.py:38
  71.6 148.2 %reduce-scatter.9.cloned.1.call-start = ((), (), s32[]{:S(2)}) async-start(), calls=%async_computation.5 | async-start | bytes 1114112 | tf_op jit(solution)/shard_map/reduce_scatter | solution.py:48
  150.8 5.2 copy-start
  156.0 285.8 %reduce-scatter.7.cloned.1.call-start = ((), (), s32[]{:S(2)}) async-start(), calls=%async_computation.4 | async-start | bytes 2162688 | tf_op jit(solution)/shard_map/reduce_scatter | solution.py:41
  184.8 257.1 %copy-start.2 = (f32[64,256]{1,0:T(8,128)S(1)}, f32[64,256]{1,0:T(8,128)}, u32[]{:S(2)}) copy-start(f32[64,256]{1,0:T(8,128)} %param.10) | copy-start | bytes 196612
  184.8 543.2 %copy-start.1 = (f32[256,256]{1,0:T(8,128)S(1)}, f32[256,256]{1,0:T(8,128)}, u32[]{:S(2)}) copy-start(f32[256,256]{1,0:T(8,128)} %param.8) | copy-start | bytes 786436
  186.7 538.6 %all-reduce.3.cloned.1.call-start = ((), (), s32[]{:S(2)}) async-start(), calls=%async_computation.3 | async-start | bytes 524288 | tf_op jit(solution)/shard_map/psum | solution.py:54
Sparse Core Ops, SparseCore 0:
  71.7 79.0 all-gather.1
  156.1 63.5 reduce-scatter.8
  224.1 217.6 reduce-scatter.6
  447.2 278.0 all-reduce.2
where the time goes:
time: 741 us; the launch traced here: 740 us
  waiting for transfers between devices  615 us (83%)
  other arithmetic  57.7 us (8%)
  blocking collectives  25.2 us (3%)
  matrix products  16.5 us (2%)
  between operations  15.3 us (2%)
  local copies, waits for them, and re-layouts  10.7 us (1%)
    psum x1, waiting for transfers between devices, body(): lax.psum(jnp.dot(trail.T, panel_exact, precision=highest), ('row', 'col'))  280 us
    reduce_scatter x1, waiting for transfers between devices, body(): lax.psum_scatter(jnp.dot(strip, panel_cols, preferred_element_type=jnp.fl...  222 us
    all_gather x1, waiting for transfers between devices, body(): panel_rows = lax.all_gather(panel_own, 'col', axis=0, tiled=True)  79.2 us
    another operation x6, other arithmetic, body(): l11 = jnp.linalg.cholesky(a11)  33.9 us
    reduce_scatter x1, waiting for transfers between devices, body(): lax.psum_scatter(inner_rows(strip, panel_rows), 'row', scatter_dimension=...  33 us
    all_gather x1, blocking collectives, body(): panel_cols = lax.all_gather(panel_own, 'row', axis=0, tiled=True)  25.2 us
    another operation x5, other arithmetic, right_solve_t(): lax.linalg.triangular_solve(factor, rhs, left_side=False, lower=True, tra...  20.3 us
  transfers between devices with their start and end apart: 4, of which 4 were waited for; matrix products, arithmetic and copies ran while one was open for 1% of the time, Pallas kernels for 0%

commit v1 on v0

--- a/solution.py
+++ b/solution.py
@@ -35,7 +35,9 @@
     l11 = jnp.linalg.cholesky(a11)
     l21_own = right_solve_t(l11, a21)
     panel_own = l21_own.astype(jnp.bfloat16)
-    panel_rows = lax.all_gather(panel_own, "col", axis=0, tiled=True)
+    panel_rows = jnp.concatenate(
+        lax.all_to_all(jnp.stack([panel_own] * lax.axis_size("col")), "col", 0, 0), axis=0
+    )
     panel_cols = lax.all_gather(panel_own, "row", axis=0, tiled=True)
     strip = tile
     row_share = lax.psum_scatter(

time: 741 us -> 694 us (0.937)
  waiting for transfers between devices: 615 us -> 533 us
  blocking collectives: 25.2 us -> 60.5 us
    all_gather x1 -> x0, waiting for transfers between devices: 79.2 us -> none  [body(): panel_rows = lax.all_gather(panel_own, 'col', axis=0, tiled=True)]
    all_to_all x0 -> x1, blocking collectives: none -> 34.2 us  [body(): lax.all_to_all(jnp.stack([panel_own] * lax.axis_size('col')), 'col', 0, 0)]
  transfers between devices with their start and end apart: 4 -> 3, of which waited for: 4 -> 3; matrix products, arithmetic and copies ran while one was open for 1% -> 1% of each run, Pallas kernels for 0% -> 0%
where the time goes in v1:
time: 694 us
  waiting for transfers between devices  533 us (77%)
  blocking collectives  60.5 us (9%)
  other arithmetic  57.1 us (8%)
  matrix products  16.2 us (2%)
  between operations  15.4 us (2%)
  local copies, waits for them, and re-layouts  11 us (2%)
    psum x1, waiting for transfers between devices, body(): lax.psum(jnp.dot(trail.T, panel_exact, precision=highest), ('row', 'col'))  280 us
    reduce_scatter x1, waiting for transfers between devices, body(): lax.psum_scatter(jnp.dot(strip, panel_cols, preferred_element_type=jnp.fl...  222 us
    all_to_all x1, blocking collectives, body(): lax.all_to_all(jnp.stack([panel_own] * lax.axis_size('col')), 'col', 0, 0)  34.2 us
    another operation x6, other arithmetic, body(): l11 = jnp.linalg.cholesky(a11)  34 us
    reduce_scatter x1, waiting for transfers between devices, body(): lax.psum_scatter(inner_rows(strip, panel_rows), 'row', scatter_dimension=...  30.7 us
    all_gather x1, blocking collectives, body(): panel_cols = lax.all_gather(panel_own, 'row', axis=0, tiled=True)  26.3 us
    another operation x5, other arithmetic, right_solve_t(): lax.linalg.triangular_solve(factor, rhs, left_side=False, lower=True, tra...  19.7 us
  transfers between devices with their start and end apart: 3, of which 3 were waited for; matrix products, arithmetic and copies ran while one was open for 1% of the time, Pallas kernels for 0%

profile of v1, /device:TPU:23, one launch (start us, length us, event | category | flops | bytes accessed | tf_op | source)
XLA Modules:
  0.0 693.5 jit_solution(13484699020758459778)
XLA Ops:
  7.2 1.1 copy.13
  8.3 1.0 fusion.4
  9.3 11.7 %cholesky.50 = f32[128,128]{1,0:T(8,128)S(1)} custom-call(f32[128,128]{1,0:T(8,128)S(1)} %cholesky.118), custom_call_target="Cholesky" | custom-call | tf_op jit(solution)/shard_map/jit(cholesky)/cholesky | solution.py:35
  21.1 9.8 %custom-call.21 = f32[1,128,128]{1,2,0:T(8,128)S(1)} custom-call(f32[1,128,128]{2,1,0:T(8,128)S(1)} %get-tuple-element.40), custom_call_target="InvertDiagBlocksLowerTriangular" | custom-call | tf_op jit(solution)/shard_map/jit(cholesky)/cholesky | solution.py:35
  30.9 0.2 constant_dynamic-update-slice_fusion.1
  31.1 0.3 convolution_subtract_fusion.3
  31.4 11.7 %cholesky.105 = f32[128,128]{1,0:T(8,128)S(1)} custom-call(f32[128,128]{1,0:T(8,128)S(1)} %convolution_subtract_fusion.3), custom_call_target="Cholesky" | custom-call | tf_op jit(solution)/shard_map/jit(cholesky)/cholesky | solution.py:35
  43.1 0.7 compare_reduce_fusion
  45.3 0.1 triangular_solve.101
  45.3 4.2 while.5
  45.5 0.6 fusion.56
  46.1 1.4 bitcast_dynamic-update-slice_fusion.2
  47.5 0.6 fusion.56
  48.1 1.4 bitcast_dynamic-update-slice_fusion.2
  49.6 19.7 %custom-call.22 = f32[2,128,128]{1,2,0:T(8,128)S(1)} custom-call(f32[2,128,128]{2,1,0:T(8,128)S(1)} %get-tuple-element.18), custom_call_target="InvertDiagBlocksLowerTriangular" | custom-call | tf_op jit(solution)/shard_map/triangular_solve | solution.py:13
  69.2 0.9 fusion.23
  70.2 1.0 convolution_subtract_fusion.5
  71.2 0.2 convolution_convert_fusion
  71.4 0.1 stack.2
  71.5 34.2 %all_to_all.5 = bf16[32,64,256]{2,1,0:T(8,128)(2,1)S(1)} all-to-all(bf16[32,64,256]{2,1,0:T(8,128)(2,1)S(1)} %stack.2), channel_id=1, replica_groups=mesh['row'=16,'col'=32] {'col'}, dimensions={0} | all-to-all | bytes 2097152 | tf_op jit(solution)/shard_map/all_to_all | solution.py:39
  105.7 3.5 convolution_bitcast_fusion.1
  109.2 1.3 copy.19
  110.6 26.3 %all_gather.3 = bf16[1024,256]{1,0:T(8,128)(2,1)S(1)} all-gather(bf16[64,256]{1,0:T(8,128)(2,1)S(1)} %pad_maximum_fusion.4), channel_id=1, replica_groups=mesh['row'=16,'col'=32] {'row'}, dimensions={0}, use_global_device_ids=true | all-gather | bytes 557056 | tf_op jit(solution)/shard_map/all_gather | solution.py:41
  136.9 3.5 convolution_bitcast_fusion
  140.5 1.9 copy.17
  142.4 30.7 %reduce-scatter.9.cloned.1.call-done = f32[64,256]{1,0:T(8,128)} async-done(((f32[1024,256]{1,0:T(8,128)}), f32[64,256]{1,0:T(8,128)}) %reduce-scatter.9.cloned.1.call-update) | async-done | bytes 65552 | tf_op jit(solution)/shard_map/reduce_scatter | solution.py:50
  173.1 221.8 %reduce-scatter.7.cloned.1.call-done = f32[64,256]{1,0:T(8,128)} async-done(((f32[2048,256]{1,0:T(8,128)}), f32[64,256]{1,0:T(8,128)}) %reduce-scatter.7.cloned.1.call-update) | async-done | bytes 65552 | tf_op jit(solution)/shard_map/reduce_scatter | solution.py:43
  394.9 0.9 subtract_subtract_fusion
  395.8 1.0 fusion.36
  396.9 0.2 fusion.24
  397.1 0.2 convolution_subtract_fusion.4
  397.3 0.2 fusion.22
  397.6 0.6 pad_maximum_fusion.3
  398.2 280.4 %all-reduce.3.cloned.1.call-done = f32[256,256]{1,0:T(8,128)} async-done(((f32[256,256]{1,0:T(8,128)}), f32[256,256]{1,0:T(8,128)}) %all-reduce.3.cloned.1.call-update) | async-done | bytes 262160 | tf_op jit(solution)/shard_map/psum | solution.py:56
  678.6 1.2 fusion.11
  679.8 1.2 convolution_subtract_fusion.2
  681.0 0.3 fusion.19
  681.3 0.5 fusion
  681.8 2.3 gather_fusion
  684.2 0.1 multiply_subtract_fusion
  684.3 0.3 fusion.9
  684.5 0.3 convolution_subtract_fusion.1
  684.8 0.3 fusion.20
  685.1 0.3 fusion.7
  685.4 0.4 convolution_subtract_fusion
  685.8 0.3 fusion.21
  686.1 0.1 copy.16
  686.2 0.7 fusion.3
  (23 shorter events, 0.4 us)
Async XLA Ops:
  7.2 166.0 %reduce-scatter.9.cloned.1.call-start = ((), (), s32[]{:S(2)}) async-start(), calls=%async_computation.5 | async-start | bytes 1114112 | tf_op jit(solution)/shard_map/reduce_scatter | solution.py:50
  110.5 284.4 %reduce-scatter.7.cloned.1.call-start = ((), (), s32[]{:S(2)}) async-start(), calls=%async_computation.4 | async-start | bytes 2162688 | tf_op jit(solution)/shard_map/reduce_scatter | solution.py:43
  140.4 254.5 %copy-start.1 = (f32[64,256]{1,0:T(8,128)S(1)}, f32[64,256]{1,0:T(8,128)}, u32[]{:S(2)}) copy-start(f32[64,256]{1,0:T(8,128)} %param.10) | copy-start | bytes 196612
  140.4 540.8 %copy-start = (f32[256,256]{1,0:T(8,128)S(1)}, f32[256,256]{1,0:T(8,128)}, u32[]{:S(2)}) copy-start(f32[256,256]{1,0:T(8,128)} %param.8) | copy-start | bytes 786436
  142.4 536.3 %all-reduce.3.cloned.1.call-start = ((), (), s32[]{:S(2)}) async-start(), calls=%async_computation.3 | async-start | bytes 524288 | tf_op jit(solution)/shard_map/psum | solution.py:56
Sparse Core Ops, SparseCore 0:
  110.6 62.4 reduce-scatter.8
  177.5 217.3 reduce-scatter.6
  400.5 278.0 all-reduce.2
